TPU v7x, 256 devices: a whole 4x4x8 slice. The times are simulated.
256 devices in a mesh: dp: 8 (over x, core), seq: 32 (over y, z).
Axes of the slice: x: 4, y: 4, z: 8, core: 2. Of those that a mesh axis runs over, the one named last changes fastest.
Arguments:
- voxels: bfloat16 [8, 4096, 4096], P('dp', 'seq'), may hold values from -6 to 6
- patch_weight: bfloat16 [4096, 1024], replicated, may hold values from -0.09375 to 0.09375
- patch_bias: float32 [1024], replicated, may hold values from -3 to 3
- enc_position: bfloat16 [4096, 1024], P('seq'), may hold values from -5 to 5
- visible: int32 [8, 4096], P('dp', 'seq'), may hold values from 0 to 1, as said below
- enc_project: bfloat16 [1024, 3072], P(('dp', 'seq')), may hold values from -1 to 1
- enc_merge: bfloat16 [1024, 1024], P(('dp', 'seq')), may hold values from -0.1875 to 0.1875
- dec_lift: bfloat16 [1024, 512], P(('dp', 'seq')), may hold values from -0.1875 to 0.1875
- mask_token: float32 [512], replicated, may hold values from -4 to 4
- dec_position: bfloat16 [4096, 512], P('seq'), may hold values from -5 to 5
- dec_project: bfloat16 [512, 1536], P(('dp', 'seq')), may hold values from -1 to 1
- dec_merge: bfloat16 [512, 512], P(('dp', 'seq')), may hold values from -0.25 to 0.25
- dec_predict: bfloat16 [512, 4096], P(('dp', 'seq')), may hold values from -0.25 to 0.25
Outputs:
- decoded: bfloat16 [8, 4096, 512], P('dp', 'seq')
- patch_loss: float32 [8, 4096], P('dp', 'seq')
Inputs may be any that keep to these rules, and one draw needn't show every extreme that they name: `visible`: each cube has exactly 1024 ones. Each slab of 128 consecutive patches holds between 0 and 64 ones, and in every cube some slab holds exactly 64.
All inputs are finite; a program needn't handle non-finite values.
Results may differ from a plain program's by a relative error of at most 0.008.
Values may be sent and summed in bfloat16 or wider, within the bound.
No kernel may reach another device: no remote copies, remote signals or barrier semaphores. Data moves between devices by JAX's collectives and lax.ppermute only.
A program may use at most 128 MiB of HBM per device.

v0:
```python
import math
import jax
import jax.numpy as jnp
from jax import lax
from jax.sharding import PartitionSpec as P

ENC_HEADS = 16
DEC_HEADS = 16


def layer_norm(values):
    centre = values - jnp.mean(values, axis=-1, keepdims=True)
    spread = jnp.mean(centre * centre, axis=-1, keepdims=True)
    return centre * lax.rsqrt(spread + 1e-06)


def attend_rows(queries, key_rows, value_rows, key_ok):
    query_rows, local_heads, head_size = queries.shape
    block_rows = math.gcd(query_rows, 512)
    score_scale = 1.0 / math.sqrt(head_size)
    query_blocks = queries[:, 0].reshape(query_rows // block_rows, block_rows, head_size)
    keys_one = key_rows[:, 0]
    values_one = value_rows[:, 0]

    def one_block(query_block):
        scores = (
            jnp.einsum("qd,kd->qk", query_block, keys_one, preferred_element_type=jnp.float32)
            * score_scale
        )
        if key_ok is not None:
            scores = jnp.where(key_ok[None, :], scores, -1e30)
        top_score = jnp.max(scores, axis=-1, keepdims=True)
        exponent = jnp.exp(scores - top_score)
        weights = (exponent / jnp.sum(exponent, axis=-1, keepdims=True)).astype(jnp.bfloat16)
        return jnp.einsum(
            "qk,kd->qd", weights, values_one, preferred_element_type=jnp.float32
        ).astype(jnp.bfloat16)

    head_outputs = [lax.map(one_block, query_blocks).reshape(query_rows, head_size)]
    return jnp.stack(head_outputs, axis=1)


def spread_heads(packed, heads, seq_count):
    row_count = packed.shape[0]
    head_size = packed.shape[1] // (3 * heads)
    query_parts = max(seq_count // heads, 1)
    local_heads = max(heads // seq_count, 1)
    layout = packed.reshape(row_count, 3, heads, head_size)
    layout = jnp.repeat(layout, query_parts, axis=2)
    layout = layout.reshape(row_count, 3, seq_count, local_heads, head_size).transpose(
        2, 1, 0, 3, 4
    )
    return layout.reshape(seq_count, 3, row_count, local_heads * head_size)


def attend_heads(incoming, key_ok, heads, query_part, query_parts):
    sources, _, row_count, piece_width = incoming.shape
    local_heads = max(heads // sources, 1)
    head_size = piece_width // local_heads
    all_rows = sources * row_count
    thirds = [incoming[:, third].reshape(all_rows, local_heads, head_size) for third in range(3)]
    query_rows = all_rows // query_parts
    queries = lax.dynamic_slice_in_dim(thirds[0], query_part * query_rows, query_rows, 0)
    return attend_rows(queries, thirds[1], thirds[2], key_ok)


def place_rows(mixed_part, all_rows, query_part, sources):
    query_rows = mixed_part.shape[0]
    flat_part = mixed_part.reshape(query_rows, -1)
    buffer = jnp.zeros((all_rows, flat_part.shape[1]), jnp.bfloat16)
    buffer = lax.dynamic_update_slice(buffer, flat_part, (query_part * query_rows, 0))
    return buffer.reshape(sources, all_rows // sources, flat_part.shape[1])


def collect_heads(returned, heads, query_parts):
    sources, row_count, piece_width = returned.shape
    local_heads = max(heads // sources, 1)
    head_size = piece_width // local_heads
    arranged = returned.reshape(sources, row_count, local_heads, head_size).transpose(1, 0, 2, 3)
    arranged = arranged.reshape(row_count, heads, query_parts, head_size)
    summed = jnp.sum(arranged.astype(jnp.float32), axis=2).astype(jnp.bfloat16)
    return summed.reshape(row_count, heads * head_size)


def send_blocks(packed, heads, seq_count):
    row_count = packed.shape[0]
    head_size = packed.shape[1] // (3 * heads)
    query_parts = seq_count // heads
    part_rows = row_count // query_parts
    layout = packed.reshape(row_count, 3, heads, head_size)
    queries = layout[:, 0].reshape(query_parts, part_rows, heads, head_size).transpose(2, 0, 1, 3)
    queries = queries.reshape(seq_count, 1, part_rows, head_size)
    pairs = (
        layout[:, 1:].transpose(2, 1, 0, 3).reshape(heads, 2 * query_parts, part_rows, head_size)
    )
    pairs = jnp.broadcast_to(pairs[:, None], (heads, query_parts) + pairs.shape[1:])
    pairs = pairs.reshape(seq_count, 2 * query_parts, part_rows, head_size)
    return jnp.concatenate([queries, pairs], axis=1)


def attend_blocks(incoming, key_ok):
    sources, blocks, part_rows, head_size = incoming.shape
    query_parts = (blocks - 1) // 2
    queries = incoming[:, 0].reshape(sources * part_rows, 1, head_size)
    keys = incoming[:, 1 : 1 + query_parts].reshape(-1, 1, head_size)
    values = incoming[:, 1 + query_parts :].reshape(-1, 1, head_size)
    mixed = attend_rows(queries, keys, values, key_ok)
    return mixed.reshape(sources, part_rows, head_size)


def take_blocks(returned, heads):
    seq_count, part_rows, head_size = returned.shape
    query_parts = seq_count // heads
    arranged = returned.reshape(heads, query_parts, part_rows, head_size).transpose(1, 2, 0, 3)
    return arranged.reshape(query_parts * part_rows, heads * head_size)


def gather_weights(pieces):
    flat = jnp.concatenate([piece.reshape(-1) for piece in pieces])
    every = lax.all_gather(flat, ("dp", "seq"), axis=0, tiled=True)
    lane = 128
    sources = every.shape[0] // flat.shape[0]
    tiles = every.reshape(sources, flat.shape[0] // lane, lane)
    wholes = []
    start = 0
    for piece in pieces:
        size = piece.size
        part = tiles[:, start // lane : (start + size) // lane, :]
        wholes.append(part.reshape(sources * piece.shape[0], piece.shape[1]))
        start += size
    return wholes


def weight_dot(rows, weight):
    return jnp.dot(rows, weight, preferred_element_type=jnp.float32)


def shards(
    voxels,
    patch_weight,
    patch_bias,
    enc_position,
    visible,
    enc_project,
    enc_merge,
    dec_lift,
    mask_token,
    dec_position,
    dec_project,
    dec_merge,
    dec_predict,
):
    seq_count = lax.axis_size("seq")
    seq_place = lax.axis_index("seq")
    enc_parts = max(seq_count // ENC_HEADS, 1)
    dec_parts = max(seq_count // DEC_HEADS, 1)
    enc_part = seq_place % enc_parts
    dec_part = seq_place % dec_parts
    project_rows, project_width = enc_project.shape
    tile_rows = 2 * project_rows
    partner = lax.ppermute(
        enc_project, "seq", perm=[(place, place ^ 1) for place in range(seq_count)]
    )
    half = seq_place % 2
    tile_block = jnp.where(
        half == 0,
        jnp.concatenate([enc_project, partner], axis=0),
        jnp.concatenate([partner, enc_project], axis=0),
    )
    own_width = project_width // 2
    own_block = lax.dynamic_slice_in_dim(tile_block, half * own_width, own_width, axis=1)
    own_block = (
        own_block.reshape(tile_rows, own_width // 128, 128).transpose(1, 0, 2).reshape(-1, 128)
    )
    tiled_project, full_merge, full_lift, *dec_weights = gather_weights(
        (own_block, enc_merge, dec_lift, dec_project, dec_merge, dec_predict)
    )
    full_project = (
        tiled_project.reshape(-1, 2, own_width // 128, tile_rows, 128)
        .transpose(0, 3, 1, 2, 4)
        .reshape(-1, project_width)
    )
    tok_local = voxels.shape[1]
    slab_max = tok_local // 2
    slot_ids = jnp.arange(slab_max, dtype=jnp.int32)
    cube_index = 0
    cube_flags = visible[cube_index]
    embedded = (
        jnp.dot(voxels[cube_index], patch_weight, preferred_element_type=jnp.float32)
        + patch_bias
        + enc_position.astype(jnp.float32)
    ).astype(jnp.bfloat16)
    ranking = jnp.cumsum(cube_flags) - 1
    slot_index = jnp.where(cube_flags == 1, ranking, slab_max)
    chooser = (slot_index[None, :] == slot_ids[:, None]).astype(jnp.bfloat16)
    kept_rows = jnp.dot(chooser, embedded, preferred_element_type=jnp.float32).astype(jnp.bfloat16)
    present = slot_ids < jnp.sum(cube_flags)
    packed = weight_dot(
        layer_norm(kept_rows.astype(jnp.float32)).astype(jnp.bfloat16), full_project
    ).astype(jnp.bfloat16)
    key_marks = jnp.broadcast_to(present.astype(jnp.bfloat16)[None, :], (seq_count, slab_max))
    outgoing = send_blocks(packed, ENC_HEADS, seq_count)
    incoming = lax.all_to_all(outgoing, "seq", split_axis=0, concat_axis=0, tiled=True)
    incoming, full_merge, full_lift, dec_weights[0] = lax.optimization_barrier(
        (incoming, full_merge, full_lift, dec_weights[0])
    )
    in_marks = lax.all_to_all(key_marks, "seq", split_axis=0, concat_axis=0, tiled=True)
    key_ok = in_marks.reshape(-1) > 0.5
    returning = attend_blocks(incoming, key_ok)
    returned = lax.all_to_all(returning, "seq", split_axis=0, concat_axis=0, tiled=True)
    mixed_rows = take_blocks(returned, ENC_HEADS)
    encoded = kept_rows.astype(jnp.float32) + weight_dot(mixed_rows, full_merge)
    lifted_list = [weight_dot(layer_norm(encoded).astype(jnp.bfloat16), full_lift)]
    rank_list = [ranking]
    cube_index = 0
    cube_flags = visible[cube_index]
    taken_rows = jnp.take(
        lifted_list[cube_index], jnp.clip(rank_list[cube_index], 0, slab_max - 1), axis=0
    )
    dec_in = (
        jnp.where(cube_flags[:, None] == 1, taken_rows, mask_token[None, :])
        + dec_position.astype(jnp.float32)
    ).astype(jnp.bfloat16)
    dec_packed = weight_dot(
        layer_norm(dec_in.astype(jnp.float32)).astype(jnp.bfloat16), dec_weights[0]
    ).astype(jnp.bfloat16)
    outgoing = send_blocks(dec_packed, DEC_HEADS, seq_count)
    incoming = lax.all_to_all(outgoing, "seq", split_axis=0, concat_axis=0, tiled=True)
    incoming, dec_weights[1], dec_weights[2] = lax.optimization_barrier(
        (incoming, dec_weights[1], dec_weights[2])
    )
    returning = attend_blocks(incoming, None)
    returned = lax.all_to_all(returning, "seq", split_axis=0, concat_axis=0, tiled=True)
    mixed_rows = take_blocks(returned, DEC_HEADS)
    decoded = (dec_in.astype(jnp.float32) + weight_dot(mixed_rows, dec_weights[1])).astype(
        jnp.bfloat16
    )
    predicted = weight_dot(
        layer_norm(decoded.astype(jnp.float32)).astype(jnp.bfloat16), dec_weights[2]
    )
    target = layer_norm(voxels[cube_index].astype(jnp.float32))
    squared = jnp.mean((predicted - target) * (predicted - target), axis=-1)
    loss_list = [jnp.where(cube_flags == 1, jnp.zeros_like(squared), squared)]
    decoded_list = [decoded]
    return (jnp.stack(decoded_list), jnp.stack(loss_list))


def solution(mesh):
    return jax.shard_map(
        shards,
        mesh=mesh,
        in_specs=(
            P("dp", "seq", None),
            P(),
            P(),
            P("seq", None),
            P("dp", "seq"),
            P(("dp", "seq"), None),
            P(("dp", "seq"), None),
            P(("dp", "seq"), None),
            P(),
            P("seq", None),
            P(("dp", "seq"), None),
            P(("dp", "seq"), None),
            P(("dp", "seq"), None),
        ),
        out_specs=(P("dp", "seq", None), P("dp", "seq")),
        check_vma=False,
    )
```

profile of v0, /device:TPU:32, one launch (start us, length us, event | category | flops | bytes accessed | tf_op | source)
XLA Modules:
  0.0 296.1 jit_solution(1052979018624724954)
XLA Ops:
  7.2 1.9 collective-permute-start
  18.4 10.7 %all-to-all-start = ((bf16[32,1,64]{2,1,0:T(2,128)(2,1)}), bf16[32,1,64]{2,1,0:T(2,128)(2,1)S(1)}, u32[]{:S(2)}, u32[]{:S(2)}) async-start(bf16[32,1,64]{2,1,0:T(2,128)(2,1)} %broadcast_in_dim.99), calls=%async_computation | async-start | bytes 32768 | tf_op jit(solution)/shard_map/all_to_all | solution.py:207
  29.2 5.2 %fusion.68 = (f32[64]{0:T(128)S(1)}, f32[64,1024]{1,0:T(8,128)S(1)}) fusion(bf16[4096,1024]{1,0:T(8,128)(2,1)} %param.18, bf16[1,128,4096]{2,1,0:T(8,128)(2,1)} %param.17, bf16[128,1024]{1,0:T(8,128)(2,1)} %param.20, f32[1024]{0:T(1024)} %param.19, s32[128]{0:T(128)S(1)} %get-tuple-element.118), kind=kOutput, calls=%fused_computation.125 | convolution fusion | flops 1091248128 | bytes 9966336 | tf_op jit(solution)/shard_map/dot_general | solution.py:196
  34.6 105.6 %all-gather.2.cloned.1.call-done = bf16[7864320]{0:T(1024)(128)(2,1)} async-done(((bf16[30720]{0:T(1024)(128)(2,1)}), bf16[7864320]{0:T(1024)(128)(2,1)}) %all-gather.2.cloned.1.call-update) | async-done | bytes 15728656 | tf_op jit(solution)/shard_map/all_gather | solution.py:120
  140.1 4.0 %slice.66 = bf16[256,96,128]{2,1,0:T(8,128)(2,1)S(1)} slice(bf16[256,240,128]{2,1,0:T(8,128)(2,1)} %bitcast.143), slice={[0:256], [0:96], [0:128]} | slice | bytes 12582912 | tf_op jit(solution)/shard_map/slice | solution.py:128
  146.8 1.6 reshape.253
  148.3 7.4 %all-to-all-start.1 = ((bf16[32,2,5120]{2,1,0:T(2,128)(2,1)}), bf16[32,2,5120]{2,1,0:T(2,128)(2,1)S(1)}, u32[]{:S(2)}, u32[]{:S(2)}) async-start(bf16[32,2,5120]{2,1,0:T(2,128)(2,1)} %reshape.253), calls=%async_computation.1 | async-start | bytes 1310720 | tf_op jit(solution)/shard_map/all_to_all | solution.py:203
  157.2 3.3 %slice.69 = bf16[256,32,128]{2,1,0:T(8,128)(2,1)} slice(bf16[256,240,128]{2,1,0:T(8,128)(2,1)} %bitcast.144), slice={[0:256], [96:128], [0:128]} | slice | bytes 4194304 | tf_op jit(solution)/shard_map/slice | solution.py:128
  160.5 2.9 slice.71
  163.4 2.4 slice.70
  165.8 2.8 reshape.229
  168.6 4.3 %reshape.231 = bf16[512,1536]{1,0:T(8,128)(2,1)} reshape(bf16[256,24,128]{2,1,0:T(8,128)(2,1)} %slice.71) | data formatting | bytes 3145728 | tf_op jit(solution)/shard_map/reshape | solution.py:129
  172.9 2.5 reshape.230
  176.5 1.8 reshape.254
  178.4 2.1 fusion.66
  181.4 7.4 %while.20 = (s32[]{:T(128)}, bf16[2,512,64]{1,2,0:T(8,128)(2,1)}, pred[2048]{0:T(1024)(128)(4,1)S(1)}, bf16[2,512,64]{2,1,0:T(8,128)(2,1)S(1)}, bf16[2048,64]{1,...) while((s32[]{:T(128)}, bf16[2,512,64]{1,2,0:T(8,128)(2,1)}, pred[2048]{0:T(1024)(128)(4,1)S(1)}, ...), condition=%wide.region_7.8_spmd, body=%wide.region_4.7_spmd.sunk | while | flops 281050112 | bytes 15941801 | solution.py:39
  190.8 8.8 %all-to-all-start.2 = ((bf16[32,2,1024]{2,1,0:T(2,128)(2,1)}), bf16[32,2,1024]{2,1,0:T(2,128)(2,1)S(1)}, u32[]{:S(2)}, u32[]{:S(2)}) async-start(bf16[32,2,1024]{2,1,0:T(2,128)(2,1)} %reshape.255), calls=%async_computation.2 | async-start | bytes 262144 | tf_op jit(solution)/shard_map/all_to_all | solution.py:210
  199.6 9.7 %all-to-all-done.2 = bf16[32,2,1024]{2,1,0:T(2,128)(2,1)S(1)} async-done(((bf16[32,2,1024]{2,1,0:T(2,128)(2,1)}), bf16[32,2,1024]{2,1,0:T(2,128)(2,1)S(1)}, u32[]{:S(2)}, u32[]{:S(2)}) %all-to-all-start.2) | async-done | bytes 131104 | tf_op jit(solution)/shard_map/all_to_all | solution.py:210
  210.7 1.7 fusion.45
  216.1 1.5 reshape.257
  217.6 4.4 %all-to-all-start.3 = ((bf16[32,2,5120]{2,1,0:T(2,128)(2,1)}), bf16[32,2,5120]{2,1,0:T(2,128)(2,1)S(1)}, u32[]{:S(2)}, u32[]{:S(2)}) async-start(bf16[32,2,5120]{2,1,0:T(2,128)(2,1)} %reshape.257), calls=%async_computation.3 | async-start | bytes 1310720 | tf_op jit(solution)/shard_map/all_to_all | solution.py:228
  222.2 5.2 %slice.75 = bf16[256,64,128]{2,1,0:T(8,128)(2,1)} slice(bf16[256,240,128]{2,1,0:T(8,128)(2,1)} %bitcast.147), slice={[0:256], [176:240], [0:128]} | slice | bytes 8388608 | tf_op jit(solution)/shard_map/slice | solution.py:128
  228.5 7.3 %reshape.238 = bf16[512,4096]{1,0:T(8,128)(2,1)} reshape(bf16[256,64,128]{2,1,0:T(8,128)(2,1)} %slice.75) | data formatting | bytes 8388608 | tf_op jit(solution)/shard_map/reshape | solution.py:129
  236.1 5.2 %all-to-all-done.3 = bf16[32,2,5120]{2,1,0:T(2,128)(2,1)S(1)} async-done(((bf16[32,2,5120]{2,1,0:T(2,128)(2,1)}), bf16[32,2,5120]{2,1,0:T(2,128)(2,1)S(1)}, u32[]{:S(2)}, u32[]{:S(2)}) %all-to-all-start.3) | async-done | bytes 655392 | tf_op jit(solution)/shard_map/all_to_all | solution.py:228
  247.8 20.5 %while.21 = (s32[]{:T(128)}, bf16[4,512,32]{1,2,0:T(8,128)(2,1)S(1)}, bf16[4,512,32]{2,1,0:T(8,128)(2,1)S(1)}, bf16[4096,32]{1,0:T(8,128)(2,1)S(1)}, bf16[4096,32]{1,0:T(8,128)(2,1)}, /*index=5*/s32[]{:T(128)}) while((s32[]{:T(128)}, bf16[4,512,32]{1,2,0:T(8,128)(2,1)S(1)}, bf16[4,512,32]{2,1,0:T(8,128)(2,1)S(1)}, ...), condition=%wide.region_15.16_spmd, body=%wide.region_12.15_spmd.sunk | while | flops 287325184 | bytes 28485736 | solution.py:39
  250.7 2.3 fusion.103
  255.8 2.3 fusion.103
  260.9 2.3 fusion.103
  266.1 2.3 fusion.103
  269.6 4.9 %all-to-all-start.4 = ((bf16[32,2,1024]{2,1,0:T(2,128)(2,1)}), bf16[32,2,1024]{2,1,0:T(2,128)(2,1)S(1)}, u32[]{:S(2)}, u32[]{:S(2)}) async-start(bf16[32,2,1024]{2,1,0:T(2,128)(2,1)} %reshape.259), calls=%async_computation.4 | async-start | bytes 262144 | tf_op jit(solution)/shard_map/all_to_all | solution.py:233
  274.9 9.2 %all-to-all-done.4 = bf16[32,2,1024]{2,1,0:T(2,128)(2,1)S(1)} async-done(((bf16[32,2,1024]{2,1,0:T(2,128)(2,1)}), bf16[32,2,1024]{2,1,0:T(2,128)(2,1)S(1)}, u32[]{:S(2)}, u32[]{:S(2)}) %all-to-all-start.4) | async-done | bytes 131104 | tf_op jit(solution)/shard_map/all_to_all | solution.py:233
  285.3 3.4 %fusion.26 = f32[128]{0:T(128)S(1)} fusion(bf16[512,4096]{1,0:T(8,128)(2,1)} %reshape.238, bf16[1,128,4096]{2,1,0:T(8,128)(2,1)S(1)} %copy-done, f32[128]{0:T(128)S(1)} %get-tuple-element.125, f32[128]{0:T(128)S(1)} %broadcast_multiply_fusion, bf16[128,512]{1,0:T(8,128)(2,1)S(1)} %get-tuple-element.124, f32[128]{0:T(128)S(1)} %get-tuple-element.126, ...), kind=kOutput, calls=%fused_computation.38 | convolution fusion | flops 540278656 | bytes 5376512 | tf_op jit(solution)/shard_map/dot_general | solution.py:135
  (148 shorter events, 52.6 us)
Async XLA Ops:
  7.2 133.0 %all-gather.2.cloned.1.call-start = ((), (), s32[]{:S(2)}) async-start(), calls=%async_computation.5 | async-start | bytes 15790080 | tf_op jit(solution)/shard_map/all_gather | solution.py:120
  7.2 4.7 %collective-permute-start = (bf16[4,3072]{1,0:T(4,128)(2,1)}, bf16[4,3072]{1,0:T(4,128)(2,1)S(1)}, u32[]{:S(2)}, u32[]{:S(2)}) collective-permute-start(bf16[4,3072]{1,0:T(4,128)(2,1)} %param.22), channel_id=1, source_target_pairs={{0,1},{1,0},{2,3},{3,2},{4,5},{5,4},{6,7},{7,6},{8,9},{9,8},{10,11... | collective-permute-start | bytes 73736 | tf_op jit(solution)/shard_map/ppermute | solution.py:161
  13.5 0.6 copy-start.11
  18.4 129.9 %all-to-all-start = ((bf16[32,1,64]{2,1,0:T(2,128)(2,1)}), bf16[32,1,64]{2,1,0:T(2,128)(2,1)S(1)}, u32[]{:S(2)}, u32[]{:S(2)}) async-start(bf16[32,1,64]{2,1,0:T(2,128)(2,1)} %broadcast_in_dim.99), calls=%async_computation | async-start | bytes 32768 | tf_op jit(solution)/shard_map/all_to_all | solution.py:207
  148.3 28.2 %all-to-all-start.1 = ((bf16[32,2,5120]{2,1,0:T(2,128)(2,1)}), bf16[32,2,5120]{2,1,0:T(2,128)(2,1)S(1)}, u32[]{:S(2)}, u32[]{:S(2)}) async-start(bf16[32,2,5120]{2,1,0:T(2,128)(2,1)} %reshape.253), calls=%async_computation.1 | async-start | bytes 1310720 | tf_op jit(solution)/shard_map/all_to_all | solution.py:203
  181.4 18.2 %copy-start.13 = (s32[128]{0:T(128)S(1)}, s32[128]{0:T(128)}, u32[]{:S(2)}) copy-start(s32[128]{0:T(128)} %get-tuple-element.84) | copy-start | bytes 1540
  181.4 18.2 %copy-start.15 = (s32[128]{0:T(128)S(1)}, s32[128]{0:T(128)}, u32[]{:S(2)}) copy-start(s32[128]{0:T(128)} %get-tuple-element.82) | copy-start | bytes 1540
  181.5 1.8 copy-start.6
  181.5 1.8 copy-start.8
  184.5 0.7 copy-start.9
  185.2 1.7 copy-start.6
  185.2 1.7 copy-start.8
  188.2 0.7 copy-start.9
  190.8 22.4 %copy-start.7 = (bf16[128,512]{1,0:T(8,128)(2,1)S(1)}, bf16[128,512]{1,0:T(8,128)(2,1)}, u32[]{:S(2)}) copy-start(bf16[128,512]{1,0:T(8,128)(2,1)} %param.26) | copy-start | bytes 393220
  190.8 22.4 %copy-start.12 = (f32[512]{0:T(512)S(1)}, f32[512]{0:T(512)}, u32[]{:S(2)}) copy-start(f32[512]{0:T(512)} %param.25) | copy-start | bytes 6148
  190.8 22.4 %copy-start.16 = (pred[128]{0:T(512)(128)(4,1)S(1)}, pred[128]{0:T(512)(128)(4,1)}, u32[]{:S(2)}) copy-start(pred[128]{0:T(512)(128)(4,1)} %fusion.64) | copy-start | bytes 388
  190.8 18.5 %all-to-all-start.2 = ((bf16[32,2,1024]{2,1,0:T(2,128)(2,1)}), bf16[32,2,1024]{2,1,0:T(2,128)(2,1)S(1)}, u32[]{:S(2)}, u32[]{:S(2)}) async-start(bf16[32,2,1024]{2,1,0:T(2,128)(2,1)} %reshape.255), calls=%async_computation.2 | async-start | bytes 262144 | tf_op jit(solution)/shard_map/all_to_all | solution.py:210
  210.5 3.5 %copy-start.1 = (bf16[512,1536]{1,0:T(8,128)(2,1)S(1)}, bf16[512,1536]{1,0:T(8,128)(2,1)}, u32[]{:S(2)}) copy-start(bf16[512,1536]{1,0:T(8,128)(2,1)} %reshape.231) | copy-start | bytes 4718596
  213.4 0.7 copy-start.2
  215.4 6.6 %copy-start = (bf16[1,128,4096]{2,1,0:T(8,128)(2,1)S(1)}, bf16[1,128,4096]{2,1,0:T(8,128)(2,1)}, u32[]{:S(2)}) copy-start(bf16[1,128,4096]{2,1,0:T(8,128)(2,1)} %param.17) | copy-start | bytes 3145732
  217.6 23.6 %all-to-all-start.3 = ((bf16[32,2,5120]{2,1,0:T(2,128)(2,1)}), bf16[32,2,5120]{2,1,0:T(2,128)(2,1)S(1)}, u32[]{:S(2)}, u32[]{:S(2)}) async-start(bf16[32,2,5120]{2,1,0:T(2,128)(2,1)} %reshape.257), calls=%async_computation.3 | async-start | bytes 1310720 | tf_op jit(solution)/shard_map/all_to_all | solution.py:228
  242.0 5.8 %copy-start.10 = (bf16[4,512,32]{1,2,0:T(8,128)(2,1)S(1)}, bf16[4,512,32]{1,2,0:T(8,128)(2,1)}, u32[]{:S(2)}) copy-start(bf16[4,512,32]{1,2,0:T(8,128)(2,1)} %custom-call.4) | copy-start | bytes 393220
  249.1 1.5 copy-start.4
  254.3 1.5 copy-start.4
  259.4 1.5 copy-start.4
  264.5 1.5 copy-start.4
  268.3 16.4 %copy-start.3 = (bf16[128,512]{1,0:T(8,128)(2,1)S(1)}, bf16[128,512]{1,0:T(8,128)(2,1)}, u32[]{:S(2)}) copy-start(bf16[128,512]{1,0:T(8,128)(2,1)} %copy-done.2) | copy-start | bytes 393220
  269.6 14.5 %all-to-all-start.4 = ((bf16[32,2,1024]{2,1,0:T(2,128)(2,1)}), bf16[32,2,1024]{2,1,0:T(2,128)(2,1)S(1)}, u32[]{:S(2)}, u32[]{:S(2)}) async-start(bf16[32,2,1024]{2,1,0:T(2,128)(2,1)} %reshape.259), calls=%async_computation.4 | async-start | bytes 262144 | tf_op jit(solution)/shard_map/all_to_all | solution.py:233
  285.1 3.6 %copy-start.5 = (bf16[128,512]{1,0:T(8,128)(2,1)}, bf16[128,512]{1,0:T(8,128)(2,1)S(1)}, u32[]{:S(2)}) copy-start(bf16[128,512]{1,0:T(8,128)(2,1)S(1)} %get-tuple-element.124) | copy-start | bytes 393220
  285.3 3.4 %copy-start.14 = (s32[1,128]{1,0:T(1,128)S(1)}, s32[1,128]{1,0:T(1,128)}, u32[]{:S(2)}) copy-start(s32[1,128]{1,0:T(1,128)} %param.21) | copy-start | bytes 1540
Sparse Core Ops, SparseCore 0:
  14.3 125.7 all-gather.1
where the time goes:
time: 298 us; the launch traced here: 296 us
  waiting for transfers between devices  131 us (44%)
  local copies, waits for them, and re-layouts  65.5 us (22%)
  starting transfers between devices  38.1 us (13%)
  matrix products  31.4 us (11%)
  other arithmetic  15.6 us (5%)
  between operations  14.6 us (5%)
    all_gather x1, waiting for transfers between devices, gather_weights(): every = lax.all_gather(flat, ('dp', 'seq'), axis=0, tiled=True)  106 us
    all_to_all x2, waiting for transfers between devices, shards(): lax.all_to_all(returning, 'seq', split_axis=0, concat_axis=0, tiled=True)  18.9 us
    slice x6, local copies, waits for them, and re-layouts, gather_weights(): part = tiles[:, start // lane:(start + size) // lane, :]  18.8 us
    reshape x5, local copies, waits for them, and re-layouts, gather_weights(): wholes.append(part.reshape(sources * piece.shape[0], piece.shape[1]))  17.2 us
    all_to_all x2, starting transfers between devices, shards(): lax.all_to_all(returning, 'seq', split_axis=0, concat_axis=0, tiled=True)  13.6 us
    all_to_all x2, starting transfers between devices, shards(): lax.all_to_all(outgoing, 'seq', split_axis=0, concat_axis=0, tiled=True)  11.8 us
    dot_general x6, matrix products, one_block(): jnp.einsum('qk,kd->qd', weights, values_one, preferred_element_type=jnp.f...  11.6 us
    all_to_all x1, starting transfers between devices, shards(): lax.all_to_all(key_marks, 'seq', split_axis=0, concat_axis=0, tiled=True)  10.7 us
  transfers between devices with their start and end apart: 7, of which 5 were waited for; matrix products, arithmetic and copies ran while one was open for 18% of the time, Pallas kernels for 0%

commit v1 on v0

--- a/solution.py
+++ b/solution.py
@@ -117,7 +117,10 @@
 
 def gather_weights(pieces):
     flat = jnp.concatenate([piece.reshape(-1) for piece in pieces])
-    every = lax.all_gather(flat, ("dp", "seq"), axis=0, tiled=True)
+    every = jnp.concatenate(
+        lax.all_to_all(jnp.stack([flat] * lax.axis_size(("dp", "seq"))), ("dp", "seq"), 0, 0),
+        axis=0,
+    )
     lane = 128
     sources = every.shape[0] // flat.shape[0]
     tiles = every.reshape(sources, flat.shape[0] // lane, lane)

time: 298 us -> 836 us (2.81); the launches traced: 296 us -> 823 us
  waiting for transfers between devices: 131 us -> 355 us
  local copies, waits for them, and re-layouts: 65.5 us -> 263 us
  other arithmetic: 15.6 us -> 107 us
  starting transfers between devices: 38.1 us -> 57.5 us
  between operations: 14.6 us -> 1.59 us
    all_to_all x0 -> x1, waiting for transfers between devices: none -> 336 us  [gather_weights(): lax.all_to_all(jnp.stack([flat] * lax.axis_size(('dp', 'seq'))), ('dp', '...]
    all_gather x1 -> x0, waiting for transfers between devices: 106 us -> none  [gather_weights(): every = lax.all_gather(flat, ('dp', 'seq'), axis=0, tiled=True)]
    another operation x1 -> x2, other arithmetic: 0.17 us -> 94 us  [the longest x1 93.8 us: gather_weights(): jnp.stack([flat] * lax.axis_size(('dp', 'seq')))]
    unnamed x41 -> x37, local copies, waits for them, and re-layouts: 10.1 us -> 103 us
    all_to_all x0 -> x1, local copies, waits for them, and re-layouts: none -> 60.5 us  [gather_weights(): lax.all_to_all(jnp.stack([flat] * lax.axis_size(('dp', 'seq'))), ('dp', '...]
    slice x6 -> x12, local copies, waits for them, and re-layouts: 18.8 us -> 44 us  [gather_weights(): part = tiles[:, start // lane:(start + size) // lane, :]]
    another operation x0 -> x2, local copies, waits for them, and re-layouts: none -> 19.1 us  [gather_weights(): jnp.stack([flat] * lax.axis_size(('dp', 'seq')))]
    all_to_all x0 -> x1, starting transfers between devices: none -> 14.7 us  [gather_weights(): lax.all_to_all(jnp.stack([flat] * lax.axis_size(('dp', 'seq'))), ('dp', '...]
  transfers between devices with their start and end apart: 7 -> 7, of which waited for: 5 -> 3; matrix products, arithmetic and copies ran while one was open for 18% -> 26% of each run, Pallas kernels for 0% -> 0%
where the time goes in v1:
time: 836 us; the launch traced here: 823 us
  waiting for transfers between devices  355 us (42%)
  local copies, waits for them, and re-layouts  263 us (31%)
  other arithmetic  107 us (13%)
  starting transfers between devices  57.5 us (7%)
  matrix products  38 us (5%)
    all_to_all x1, waiting for transfers between devices, gather_weights(): lax.all_to_all(jnp.stack([flat] * lax.axis_size(('dp', 'seq'))), ('dp', '...  336 us
    unnamed x37, local copies, waits for them, and re-layouts  103 us
    another operation x1, other arithmetic, gather_weights(): jnp.stack([flat] * lax.axis_size(('dp', 'seq')))  93.8 us
    all_to_all x1, local copies, waits for them, and re-layouts, gather_weights(): lax.all_to_all(jnp.stack([flat] * lax.axis_size(('dp', 'seq'))), ('dp', '...  60.5 us
    slice x12, local copies, waits for them, and re-layouts, gather_weights(): part = tiles[:, start // lane:(start + size) // lane, :]  44 us
    all_to_all x2, starting transfers between devices, shards(): lax.all_to_all(returning, 'seq', split_axis=0, concat_axis=0, tiled=True)  20.1 us
    reshape x5, local copies, waits for them, and re-layouts, gather_weights(): wholes.append(part.reshape(sources * piece.shape[0], piece.shape[1]))  19.3 us
    another operation x2, local copies, waits for them, and re-layouts, gather_weights(): jnp.stack([flat] * lax.axis_size(('dp', 'seq')))  19.1 us
  transfers between devices with their start and end apart: 7, of which 3 were waited for; matrix products, arithmetic and copies ran while one was open for 26% of the time, Pallas kernels for 0%

profile of v1, /device:TPU:32, one launch (start us, length us, event | category | flops | bytes accessed | tf_op | source)
XLA Modules:
  0.0 822.8 jit_solution(6684544895241375536)
XLA Ops:
  7.0 18.6 %stack.4 = bf16[256,1,30720]{2,1,0:T(2,128)(2,1)} broadcast(bf16[30720]{0:T(1024)(128)(2,1)S(1)} %constant_dynamic-update-slice_fusion), dimensions={2} | broadcast | bytes 15790080 | tf_op jit(solution)/shard_map/stack | solution.py:121
  26.1 93.8 %reduce.9 = bf16[256,30720]{1,0:T(8,128)(2,1)} reduce(bf16[256,1,30720]{2,1,0:T(2,128)(2,1)} %stack.4, bf16[]{:T(256)} %broadcast.272), dimensions={1}, to_apply=%stack.4.reduce_sub_computation | reduce | bytes 31457282 | tf_op jit(solution)/shard_map/stack | solution.py:121
  119.9 20.1 %reshape.257 = bf16[256,2,15360]{2,1,0:T(2,128)(2,1)} reshape(bf16[256,30720]{1,0:T(8,128)(2,1)} %reduce.9) | data formatting | bytes 31457280
  140.0 14.7 %all-to-all-start.1 = ((bf16[256,2,15360]{2,1,0:T(2,128)(2,1)}), bf16[256,2,15360]{2,1,0:T(2,128)(2,1)}, u32[]{:S(2)}, u32[]{:S(2)}) async-start(bf16[256,2,15360]{2,1,0:T(2,128)(2,1)} %reshape.257), calls=%async_computation.1 | async-start | bytes 31457280 | tf_op jit(solution)/shard_map/all_to_all | solution.py:121
  156.4 4.9 fusion.68
  161.5 336.4 %all-to-all-done.1 = bf16[256,2,15360]{2,1,0:T(2,128)(2,1)} async-done(((bf16[256,2,15360]{2,1,0:T(2,128)(2,1)}), bf16[256,2,15360]{2,1,0:T(2,128)(2,1)}, u32[]{:S(2)}, u32[]{:S(2)}) %all-to-all-start.1) | async-done | bytes 15728672 | tf_op jit(solution)/shard_map/all_to_all | solution.py:121
  498.6 6.5 all-to-all-start
  505.1 73.9 %reshape.258 = bf16[256,1,30720]{2,1,0:T(2,128)(2,1)} reshape(bf16[256,2,15360]{2,1,0:T(2,128)(2,1)} %all-to-all-done.1) | data formatting | bytes 31457280
  579.0 60.5 %copy.66 = bf16[256,1,30720]{0,2,1:T(8,128)(2,1)} copy(bf16[256,1,30720]{2,1,0:T(2,128)(2,1)} %reshape.258) | data formatting | bytes 31457280 | tf_op jit(solution)/shard_map/all_to_all | solution.py:121
  639.6 6.2 slice.66
  645.8 8.9 %copy.67 = bf16[256,96,128]{2,1,0:T(8,128)(2,1)} copy(bf16[256,96,128]{0,2,1:T(8,128)(2,1)} %slice.66) | data formatting | bytes 12582912 | tf_op jit(solution)/shard_map/slice | solution.py:131
  654.7 4.0 convolution_convert_fusion
  661.7 9.8 %all-to-all-start.2 = ((bf16[32,2,5120]{2,1,0:T(2,128)(2,1)}), bf16[32,2,5120]{2,1,0:T(2,128)(2,1)}, u32[]{:S(2)}, u32[]{:S(2)}) async-start(bf16[32,2,5120]{2,1,0:T(2,128)(2,1)} %reshape.259), calls=%async_computation.2 | async-start | bytes 1310720 | tf_op jit(solution)/shard_map/all_to_all | solution.py:206
  671.7 3.2 slice.69
  678.9 4.6 copy.70
  683.5 4.2 reshape.233
  690.4 4.3 reshape.235
  702.5 6.1 while.20
  709.6 10.2 %all-to-all-start.3 = ((bf16[32,2,1024]{2,1,0:T(2,128)(2,1)}), bf16[32,2,1024]{2,1,0:T(2,128)(2,1)S(1)}, u32[]{:S(2)}, u32[]{:S(2)}) async-start(bf16[32,2,1024]{2,1,0:T(2,128)(2,1)} %reshape.261), calls=%async_computation.3 | async-start | bytes 262144 | tf_op jit(solution)/shard_map/all_to_all | solution.py:213
  719.9 9.5 %all-to-all-done.3 = bf16[32,2,1024]{2,1,0:T(2,128)(2,1)S(1)} async-done(((bf16[32,2,1024]{2,1,0:T(2,128)(2,1)}), bf16[32,2,1024]{2,1,0:T(2,128)(2,1)S(1)}, u32[]{:S(2)}, u32[]{:S(2)}) %all-to-all-start.3) | async-done | bytes 131104 | tf_op jit(solution)/shard_map/all_to_all | solution.py:213
  739.1 4.5 all-to-all-start.4
  743.8 4.6 slice.75
  749.5 6.6 copy.80
  756.0 7.3 reshape.242
  772.6 23.0 %while.21 = (s32[]{:T(128)}, bf16[4,512,32]{1,2,0:T(8,128)(2,1)}, bf16[4,512,32]{2,1,0:T(8,128)(2,1)S(1)}, bf16[4096,32]{1,0:T(8,128)(2,1)S(1)}, bf16[4096,32]{1,0:T(8,128)(2,1)}, /*index=5*/s32[]{:T(128)}) while((s32[]{:T(128)}, bf16[4,512,32]{1,2,0:T(8,128)(2,1)}, bf16[4,512,32]{2,1,0:T(8,128)(2,1)S(1)}, bf16[4096,32]{1,0:T(8,128)(2,1)S(1)}, ...), condition=%wide.region_15.16_spmd, body=%wide.region_12.15_spmd.sunk | while | flops 287325184 | bytes 27699812 | solution.py:39
  775.4 2.9 fusion.103
  781.2 2.9 fusion.103
  786.9 2.9 fusion.103
  792.7 2.9 fusion.103
  797.8 9.9 %all-to-all-start.5 = ((bf16[32,2,1024]{2,1,0:T(2,128)(2,1)}), bf16[32,2,1024]{2,1,0:T(2,128)(2,1)S(1)}, u32[]{:S(2)}, u32[]{:S(2)}) async-start(bf16[32,2,1024]{2,1,0:T(2,128)(2,1)} %reshape.265), calls=%async_computation.5 | async-start | bytes 262144 | tf_op jit(solution)/shard_map/all_to_all | solution.py:236
  808.1 9.2 %all-to-all-done.5 = bf16[32,2,1024]{2,1,0:T(2,128)(2,1)S(1)} async-done(((bf16[32,2,1024]{2,1,0:T(2,128)(2,1)}), bf16[32,2,1024]{2,1,0:T(2,128)(2,1)S(1)}, u32[]{:S(2)}, u32[]{:S(2)}) %all-to-all-start.5) | async-done | bytes 131104 | tf_op jit(solution)/shard_map/all_to_all | solution.py:236
  818.5 3.4 fusion.26
  (145 shorter events, 69.7 us)
Async XLA Ops:
  0.6 4.7 collective-permute-start
  140.0 14.7 %copy-start.10 = (s32[1,128]{1,0:T(1,128)S(1)}, s32[1,128]{1,0:T(1,128)}, u32[]{:S(2)}) copy-start(s32[1,128]{1,0:T(1,128)} %param.21) | copy-start | bytes 1540
  140.0 16.4 %copy-start = (bf16[1,128,4096]{2,1,0:T(8,128)(2,1)S(1)}, bf16[1,128,4096]{2,1,0:T(8,128)(2,1)}, u32[]{:S(2)}) copy-start(bf16[1,128,4096]{2,1,0:T(8,128)(2,1)} %param.17) | copy-start | bytes 3145732
  140.0 16.4 %copy-start.6 = (bf16[128,1024]{1,0:T(8,128)(2,1)S(1)}, bf16[128,1024]{1,0:T(8,128)(2,1)}, u32[]{:S(2)}) copy-start(bf16[128,1024]{1,0:T(8,128)(2,1)} %param.20) | copy-start | bytes 786436
  140.0 16.4 %copy-start.8 = (f32[1024]{0:T(1024)S(1)}, f32[1024]{0:T(1024)}, u32[]{:S(2)}) copy-start(f32[1024]{0:T(1024)} %param.19) | copy-start | bytes 12292
  140.0 358.0 %all-to-all-start.1 = ((bf16[256,2,15360]{2,1,0:T(2,128)(2,1)}), bf16[256,2,15360]{2,1,0:T(2,128)(2,1)}, u32[]{:S(2)}, u32[]{:S(2)}) async-start(bf16[256,2,15360]{2,1,0:T(2,128)(2,1)} %reshape.257), calls=%async_computation.1 | async-start | bytes 31457280 | tf_op jit(solution)/shard_map/all_to_all | solution.py:121
  498.6 163.1 %all-to-all-start = ((bf16[32,1,64]{2,1,0:T(2,128)(2,1)}), bf16[32,1,64]{2,1,0:T(2,128)(2,1)S(1)}, u32[]{:S(2)}, u32[]{:S(2)}) async-start(bf16[32,1,64]{2,1,0:T(2,128)(2,1)} %broadcast_in_dim.99), calls=%async_computation | async-start | bytes 32768 | tf_op jit(solution)/shard_map/all_to_all | solution.py:210
  661.7 37.3 %all-to-all-start.2 = ((bf16[32,2,5120]{2,1,0:T(2,128)(2,1)}), bf16[32,2,5120]{2,1,0:T(2,128)(2,1)}, u32[]{:S(2)}, u32[]{:S(2)}) async-start(bf16[32,2,5120]{2,1,0:T(2,128)(2,1)} %reshape.259), calls=%async_computation.2 | async-start | bytes 1310720 | tf_op jit(solution)/shard_map/all_to_all | solution.py:206
  702.5 1.7 copy-start.5
  705.5 1.8 copy-start.5
  708.6 23.9 %copy-start.1 = (bf16[1024,512]{1,0:T(8,128)(2,1)S(1)}, bf16[1024,512]{1,0:T(8,128)(2,1)}, u32[]{:S(2)}) copy-start(bf16[1024,512]{1,0:T(8,128)(2,1)} %reshape.234) | copy-start | bytes 3145732
  709.6 23.9 %copy-start.7 = (bf16[128,512]{1,0:T(8,128)(2,1)S(1)}, bf16[128,512]{1,0:T(8,128)(2,1)}, u32[]{:S(2)}) copy-start(bf16[128,512]{1,0:T(8,128)(2,1)} %param.26) | copy-start | bytes 393220
  709.6 23.9 %copy-start.9 = (f32[512]{0:T(512)S(1)}, f32[512]{0:T(512)}, u32[]{:S(2)}) copy-start(f32[512]{0:T(512)} %param.25) | copy-start | bytes 6148
  709.6 19.8 %all-to-all-start.3 = ((bf16[32,2,1024]{2,1,0:T(2,128)(2,1)}), bf16[32,2,1024]{2,1,0:T(2,128)(2,1)S(1)}, u32[]{:S(2)}, u32[]{:S(2)}) async-start(bf16[32,2,1024]{2,1,0:T(2,128)(2,1)} %reshape.261), calls=%async_computation.3 | async-start | bytes 262144 | tf_op jit(solution)/shard_map/all_to_all | solution.py:213
  739.1 25.7 %all-to-all-start.4 = ((bf16[32,2,5120]{2,1,0:T(2,128)(2,1)}), bf16[32,2,5120]{2,1,0:T(2,128)(2,1)S(1)}, u32[]{:S(2)}, u32[]{:S(2)}) async-start(bf16[32,2,5120]{2,1,0:T(2,128)(2,1)} %reshape.263), calls=%async_computation.4 | async-start | bytes 1310720 | tf_op jit(solution)/shard_map/all_to_all | solution.py:231
  773.9 1.5 copy-start.3
  779.7 1.5 copy-start.3
  785.4 1.5 copy-start.3
  791.1 1.5 copy-start.3
  795.5 22.4 %copy-start.2 = (bf16[512,512]{1,0:T(8,128)(2,1)S(1)}, bf16[512,512]{1,0:T(8,128)(2,1)}, u32[]{:S(2)}) copy-start(bf16[512,512]{1,0:T(8,128)(2,1)} %reshape.241) | copy-start | bytes 1572868
  797.8 19.6 %all-to-all-start.5 = ((bf16[32,2,1024]{2,1,0:T(2,128)(2,1)}), bf16[32,2,1024]{2,1,0:T(2,128)(2,1)S(1)}, u32[]{:S(2)}, u32[]{:S(2)}) async-start(bf16[32,2,1024]{2,1,0:T(2,128)(2,1)} %reshape.265), calls=%async_computation.5 | async-start | bytes 262144 | tf_op jit(solution)/shard_map/all_to_all | solution.py:236
  818.3 3.6 copy-start.4
  818.5 3.4 copy-start.11
